TPU v7x, 512 devices: a whole 4x8x8 slice. The times are simulated.
512 devices in a mesh: seq: 64 (over y, x, core), ch: 8 (over z).
Axes of the slice: x: 4, y: 8, z: 8, core: 2. Of those that a mesh axis runs over, the one named last changes fastest.
Arguments:
- signal: bfloat16 [1536, 32768], P('ch', 'seq'), may hold values from -16 to 16
- input_norm_gain: float32 [1536], P('ch'), may hold values from 0.25 to 1.75
- value_weight: bfloat16 [1536, 1536], P('seq', 'ch'), may hold values from -0.15625 to 0.15625
- gate_weight: bfloat16 [1536, 1536], P('seq', 'ch'), may hold values from -0.15625 to 0.15625
- depth_taps: float32 [31, 1536], P(None, 'ch'), may hold values from -1 to 1
- cotangent: bfloat16 [1536, 32768], P('ch', 'seq'), may hold values from -6 to 6
Outputs:
- output: bfloat16 [1536, 32768], P('ch', 'seq')
- signal_gradient: bfloat16 [1536, 32768], P('ch', 'seq')
- grad_value: float32 [1536, 1536], P('seq', 'ch')
- grad_gate: float32 [1536, 1536], P('seq', 'ch')
- grad_taps: float32 [31, 1536], P(None, 'ch')
- gain_gradient: float32 [1536], P('ch')
All inputs are finite; a program needn't handle non-finite values.
Results may differ from a plain program's by a relative error of at most 0.02.
Values may be sent and summed in bfloat16 or wider, within the bound.
No kernel may reach another device: no remote copies, remote signals or barrier semaphores. Data moves between devices by JAX's collectives and lax.ppermute only.
A program may use at most 64 MiB of HBM per device.

v0:
```python
import jax
import jax.numpy as jnp
from jax import lax
from jax.sharding import PartitionSpec as P


def extended(cells, sides, width):
    for axis, dim in sides:
        count = lax.axis_size(axis)
        ends = count - 1
        head = lax.slice_in_dim(cells, 0, width, axis=dim)
        tail = lax.slice_in_dim(cells, cells.shape[dim] - width, cells.shape[dim], axis=dim)
        cells = jnp.concatenate(
            [
                lax.ppermute(tail, axis, [(i, (i + 1) % count) for i in range(ends)]),
                cells,
                lax.ppermute(head, axis, [((i + 1) % count, i) for i in range(ends)]),
            ],
            axis=dim,
        )
    return cells


def standardize_rows(columns_in):
    values = columns_in.astype(jnp.float32)
    average = jnp.mean(values, 0, keepdims=True)
    centred = values - average
    spread = jnp.mean(centred * centred, 0, keepdims=True)
    inverse_deviation = lax.rsqrt(spread + 1e-05)
    return (centred * inverse_deviation, inverse_deviation)


def depthwise(padded, kernel):
    channels = padded.shape[0]
    result = lax.conv_general_dilated(
        padded[None],
        kernel,
        (1,),
        "VALID",
        dimension_numbers=("NCH", "OIH", "NCH"),
        feature_group_count=channels,
        precision=lax.Precision.HIGHEST,
    )
    return result[0]


def shards(signal, input_norm_gain, value_weight, gate_weight, depth_taps, cotangent):
    local_cols = signal.shape[0]
    frames = signal.shape[1]
    groups = lax.axis_size("ch")
    block_of_rows = frames // groups
    channel_position = lax.axis_index("ch")
    reach = depth_taps.shape[0] // 2
    complete_signal, complete_gain = (
        lax.all_gather(signal, "ch", axis=0, tiled=True),
        lax.all_gather(input_norm_gain.astype(jnp.bfloat16), "ch", axis=0, tiled=True).astype(
            input_norm_gain.dtype
        ),
    )
    centered_unit, inverse_deviation = standardize_rows(complete_signal)
    normalized_signal = (centered_unit * complete_gain[:, None]).astype(jnp.bfloat16)
    centered_unit_rows = lax.dynamic_slice_in_dim(
        centered_unit, channel_position * block_of_rows, block_of_rows, 1
    )
    row_inverse_deviation = lax.dynamic_slice_in_dim(
        inverse_deviation, channel_position * block_of_rows, block_of_rows, 1
    )
    stacked = jnp.concatenate([value_weight, gate_weight], 1)
    gathered = lax.all_gather(stacked, "seq", axis=0, tiled=True)
    mixed = lax.dot_general(
        gathered, normalized_signal, (((0,), (0,)), ((), ())), preferred_element_type=jnp.float32
    )
    value = mixed[:local_cols]
    gate = mixed[local_cols:]
    sig_gate = jax.nn.sigmoid(gate)
    glued = (value * sig_gate).astype(jnp.bfloat16)
    glued_pad = extended(glued, (("seq", 1),), reach).astype(jnp.float32)
    forward_kernel = depth_taps.T[:, None, :]
    pre = depthwise(glued_pad, forward_kernel)
    sig_pre = jax.nn.sigmoid(pre)
    output = (pre * sig_pre).astype(jnp.bfloat16)
    grad_pre = (cotangent.astype(jnp.float32) * sig_pre * (1.0 + pre * (1.0 - sig_pre))).astype(
        jnp.bfloat16
    )
    grad_pre_f = grad_pre.astype(jnp.float32)
    grad_pad = extended(grad_pre, (("seq", 1),), reach).astype(jnp.float32)
    grad_glued = depthwise(grad_pad, forward_kernel[:, :, ::-1])
    tap_partial = depthwise(glued_pad, grad_pre_f[:, None, :]).T
    grad_taps = lax.psum(tap_partial, "seq")
    grad_v = (grad_glued * sig_gate).astype(jnp.bfloat16)
    grad_g = (grad_glued * value * sig_gate * (1.0 - sig_gate)).astype(jnp.bfloat16)
    grad_both = jnp.concatenate([grad_v, grad_g], 0)
    weight_sums = lax.psum_scatter(
        lax.dot_general(
            normalized_signal,
            grad_both,
            (((1,), (1,)), ((), ())),
            preferred_element_type=jnp.float32,
        ),
        "seq",
        scatter_dimension=0,
        tiled=True,
    )
    grad_value = weight_sums[:, :local_cols]
    grad_gate = weight_sums[:, local_cols:]
    normed_term = jnp.dot(gathered, grad_both, preferred_element_type=jnp.float32)
    normalized_gradient = lax.psum_scatter(
        normed_term.astype(jnp.bfloat16), "ch", scatter_dimension=1, tiled=True
    ).astype(jnp.float32)
    scaled_signal = normalized_gradient * complete_gain[:, None]
    first_moment = jnp.mean(scaled_signal, 0, keepdims=True)
    second_moment = jnp.mean(scaled_signal * centered_unit_rows, 0, keepdims=True)
    gradient_rows = (
        row_inverse_deviation * (scaled_signal - first_moment - centered_unit_rows * second_moment)
    ).astype(jnp.bfloat16)
    signal_gradient = lax.all_to_all(gradient_rows, "ch", split_axis=0, concat_axis=1, tiled=True)
    gain_portion = jnp.sum(normalized_gradient * centered_unit_rows, 1)
    gain_whole = lax.psum(gain_portion, ("seq", "ch"))
    gain_gradient = lax.dynamic_slice_in_dim(
        gain_whole, channel_position * local_cols, local_cols, 0
    )
    return (output, signal_gradient, grad_value, grad_gate, grad_taps, gain_gradient)


def solution(mesh):
    placed = (
        P("ch", "seq"),
        P("ch"),
        P("seq", "ch"),
        P("seq", "ch"),
        P(None, "ch"),
        P("ch", "seq"),
    )
    return jax.shard_map(
        shards,
        mesh=mesh,
        in_specs=placed,
        out_specs=(
            P("ch", "seq"),
            P("ch", "seq"),
            P("seq", "ch"),
            P("seq", "ch"),
            P(None, "ch"),
            P("ch"),
        ),
        check_vma=False,
    )
```

profile of v0, /device:TPU:1, one launch (start us, length us, event | category | flops | bytes accessed | tf_op | source)
XLA Modules:
  0.0 592.0 jit_solution(6644750311934210366)
XLA Ops:
  7.2 0.7 all-gather.5.cloned.1.call-update
  8.0 1.4 pad_maximum_fusion.4
  9.5 0.7 convert_element_type.43
  10.1 1.3 dynamic-slice.4
  12.1 0.2 dynamic-update-slice
  12.3 20.2 %all-reduce = bf16[1536]{0:T(1024)(128)(2,1)S(1)} all-reduce(bf16[1536]{0:T(1024)(128)(2,1)S(1)} %dynamic-update-slice), channel_id=1, replica_groups=mesh['seq'=64,'ch'=8] {'ch'}, use_global_device_ids=true, to_apply=%add | all-reduce | flops 1536 | bytes 6144
  32.6 22.6 %all-gather.5.cloned.1.call-done = bf16[1536,512]{1,0:T(8,128)(2,1)} async-done(((bf16[192,512]{1,0:T(8,128)(2,1)}), bf16[1536,512]{1,0:T(8,128)(2,1)}) %all-gather.5.cloned.1.call-update) | async-done | bytes 1572880 | tf_op jit(solution)/shard_map/all_gather | solution.py:55
  55.2 1.7 copy.41
  56.9 0.3 convert_reduce_fusion
  57.2 0.5 fusion.2
  57.8 85.3 %all-gather.3.cloned.1.call-done = bf16[1536,384]{1,0:T(8,128)(2,1)} async-done(((bf16[24,384]{1,0:T(8,128)(2,1)}), bf16[1536,384]{1,0:T(8,128)(2,1)}) %all-gather.3.cloned.1.call-update) | async-done | bytes 1179664 | tf_op jit(solution)/shard_map/all_gather | solution.py:69
  143.1 2.2 fusion.6
  145.6 2.1 collective-permute-start.1
  147.7 3.4 collective-permute-start
  151.2 1.1 collective-permute-done
  152.3 0.8 fusion.33
  153.2 0.4 reshape.83
  153.6 0.4 copy.44
  154.1 2.0 convolution_select_fusion.1
  156.1 1.4 copy.58
  157.5 1.0 reshape.80
  158.5 2.0 multiply_convert_fusion.5
  160.6 1.9 collective-permute-start.3
  162.5 4.2 collective-permute-start.2
  166.8 1.1 collective-permute-done.2
  168.1 0.4 reshape.84
  168.5 0.4 copy.50
  168.9 2.0 convolution_select_fusion
  171.0 1.4 copy.59
  172.4 1.0 reshape.81
  173.4 1.2 multiply_convert_fusion.4
  174.6 3.5 convolution_convert_fusion
  178.4 1.3 dynamic-slice.5
  180.4 2.1 fusion
  182.4 0.9 copy.55
  183.3 0.4 copy.56
  183.8 2.7 fusion.5
  186.5 38.9 %reduce-scatter.2.cloned.1.call-done = bf16[1536,64]{0,1:T(8,128)(2,1)} async-done(((bf16[1536,512]{0,1:T(8,128)(2,1)}), bf16[1536,64]{0,1:T(8,128)(2,1)}) %reduce-scatter.2.cloned.1.call-update) | async-done | bytes 196624 | tf_op jit(solution)/shard_map/reduce_scatter | solution.py:107
  225.4 1.3 fusion.26
  226.7 1.2 fusion.24
  228.2 0.7 copy.54
  228.9 4.7 all-to-all-start
  233.6 2.2 fusion.49
  235.9 245.9 %psum.14 = f32[31,192]{1,0:T(8,128)} all-reduce(f32[31,192]{1,0:T(8,128)S(1)} %bitcast.60), channel_id=1, replica_groups=mesh['seq'=64,'ch'=8] {'seq'}, use_global_device_ids=true, to_apply=%region_6.0 | all-reduce | flops 5952 | bytes 47616 | tf_op jit(solution)/shard_map/psum | solution.py:89
  481.8 1.5 fusion.46
  483.3 100.8 %psum.15 = f32[1536]{0:T(1024)S(1)} all-reduce(f32[1536]{0:T(1024)S(1)} %get-tuple-element.18), channel_id=1, replica_groups=mesh['seq'=64,'ch'=8] {'seq','ch'}, use_global_device_ids=true, to_apply=%region_8.0 | all-reduce | flops 1536 | bytes 12288 | tf_op jit(solution)/shard_map/psum | solution.py:118
  584.1 0.6 dynamic_slice.8
  584.7 0.8 copy.57
  (33 shorter events, 1.3 us)
Async XLA Ops:
  7.2 146.9 %copy-start = (f32[31,192]{1,0:T(8,128)S(1)}, f32[31,192]{1,0:T(8,128)}, u32[]{:S(2)}) copy-start(f32[31,192]{1,0:T(8,128)} %param.10) | copy-start | bytes 71428
  7.2 48.0 %all-gather.5.cloned.1.call-start = ((), (), s32[]{:S(2)}) async-start(), calls=%async_computation.3 | async-start | bytes 1769472 | tf_op jit(solution)/shard_map/all_gather | solution.py:55
  7.9 135.2 %all-gather.3.cloned.1.call-start = ((), (), s32[]{:S(2)}) async-start(), calls=%async_computation.2 | async-start | bytes 1198080 | tf_op jit(solution)/shard_map/all_gather | solution.py:69
  9.4 216.0 %reduce-scatter.2.cloned.1.call-start = ((), (), s32[]{:S(2)}) async-start(), calls=%async_computation.4 | async-start | bytes 1769472 | tf_op jit(solution)/shard_map/reduce_scatter | solution.py:107
  145.3 8.7 %copy-start.2 = (pred[8,68]{0,1:T(8,128)(4,1)S(1)}, pred[8,68]{0,1:T(8,128)(4,1)}, u32[]{:S(2)}) copy-start(pred[8,68]{0,1:T(8,128)(4,1)} %constant.43) | copy-start | bytes 1636
  145.6 5.6 collective-permute-start.1
  147.7 4.6 collective-permute-start
  160.6 6.2 %collective-permute-start.3 = (bf16[192,15]{1,0:T(8,128)(2,1)S(1)}, bf16[192,15]{1,0:T(8,128)(2,1)S(1)}, u32[]{:S(2)}, u32[]{:S(2)}) collective-permute-start(bf16[192,15]{1,0:T(8,128)(2,1)S(1)} %get-tuple-element.30), channel_id=1, source_target_pairs={{8,0},{16,8},{24,16},{32,24},{40,32},{48,40},{56,48},{64,56},{72,6... | collective-permute-start | bytes 17288 | tf_op jit(solution)/shard_map/ppermute | solution.py:17
  162.5 5.4 collective-permute-start.2
  178.1 4.3 copy-start.1
  178.1 303.6 %all-reduce.4.cloned.1.call-start = ((), (), s32[]{:S(2)}) async-start(), calls=%async_computation.5 | async-start | bytes 4718592
  228.9 355.8 %all-to-all-start = ((bf16[8,192,64]{1,2,0:T(8,128)(2,1)}), bf16[8,192,64]{1,2,0:T(8,128)(2,1)S(1)}, u32[]{:S(2)}, u32[]{:S(2)}) async-start(bf16[8,192,64]{1,2,0:T(8,128)(2,1)} %copy.54), calls=%async_computation.1 | async-start | bytes 524288 | tf_op jit(solution)/shard_map/all_to_all | solution.py:116
Sparse Core Ops, SparseCore 0:
  10.1 45.0 all-gather.4
  59.0 84.0 all-gather.2
  178.3 47.0 reduce-scatter.1
  228.6 202.0 all-reduce.3
where the time goes:
time: 593 us; the launch traced here: 592 us
  blocking collectives  367 us (62%)
  waiting for transfers between devices  150 us (25%)
  starting transfers between devices  16.8 us (3%)
  local copies, waits for them, and re-layouts  16.6 us (3%)
  between operations  15.3 us (3%)
  matrix products  14.7 us (2%)
  other arithmetic  11.8 us (2%)
    psum x1, blocking collectives, shards(): grad_taps = lax.psum(tap_partial, 'seq')  246 us
    psum x1, blocking collectives, shards(): gain_whole = lax.psum(gain_portion, ('seq', 'ch'))  101 us
    all_gather x1, waiting for transfers between devices, shards(): gathered = lax.all_gather(stacked, 'seq', axis=0, tiled=True)  85.3 us
    reduce_scatter x1, waiting for transfers between devices, shards(): lax.psum_scatter(normed_term.astype(jnp.bfloat16), 'ch', scatter_dimensio...  38.9 us
    all_gather x1, waiting for transfers between devices, shards(): lax.all_gather(signal, 'ch', axis=0, tiled=True)  22.6 us
    unnamed x1, blocking collectives  20.2 us
  transfers between devices with their start and end apart: 9, of which 5 were waited for; matrix products, arithmetic and copies ran while one was open for 4% of the time, Pallas kernels for 0%

commit v1 on v0

--- a/solution.py
+++ b/solution.py
@@ -86,7 +86,7 @@
     grad_pad = extended(grad_pre, (("seq", 1),), reach).astype(jnp.float32)
     grad_glued = depthwise(grad_pad, forward_kernel[:, :, ::-1])
     tap_partial = depthwise(glued_pad, grad_pre_f[:, None, :]).T
-    grad_taps = lax.psum(tap_partial, "seq")
+    grad_taps = jnp.sum(lax.all_gather(tap_partial, "seq"), axis=0)
     grad_v = (grad_glued * sig_gate).astype(jnp.bfloat16)
     grad_g = (grad_glued * value * sig_gate * (1.0 - sig_gate)).astype(jnp.bfloat16)
     grad_both = jnp.concatenate([grad_v, grad_g], 0)

time: 593 us -> 626 us (1.056)
  waiting for transfers between devices: 150 us -> 429 us
  blocking collectives: 367 us -> 117 us
    psum x1 -> x0, blocking collectives: 246 us -> none  [shards(): grad_taps = lax.psum(tap_partial, 'seq')]
    unnamed x5 -> x6, waiting for transfers between devices: 0.73 us -> 195 us
    all_gather x0 -> x1, waiting for transfers between devices: none -> 86 us  [shards(): grad_taps = jnp.sum(lax.all_gather(tap_partial, 'seq'), axis=0)]
  transfers between devices with their start and end apart: 9 -> 10, of which waited for: 5 -> 7; matrix products, arithmetic and copies ran while one was open for 4% -> 4% of each run, Pallas kernels for 0% -> 0%
where the time goes in v1:
time: 626 us; the launch traced here: 625 us
  waiting for transfers between devices  429 us (69%)
  blocking collectives  117 us (19%)
  local copies, waits for them, and re-layouts  17.2 us (3%)
  starting transfers between devices  16.9 us (3%)
  between operations  15.4 us (2%)
  matrix products  14.6 us (2%)
  other arithmetic  14.1 us (2%)
    unnamed x6, waiting for transfers between devices  195 us
    psum x1, blocking collectives, shards(): gain_whole = lax.psum(gain_portion, ('seq', 'ch'))  97.2 us
    all_gather x1, waiting for transfers between devices, shards(): grad_taps = jnp.sum(lax.all_gather(tap_partial, 'seq'), axis=0)  86 us
    all_gather x1, waiting for transfers between devices, shards(): gathered = lax.all_gather(stacked, 'seq', axis=0, tiled=True)  85.3 us
    reduce_scatter x1, waiting for transfers between devices, shards(): lax.psum_scatter(normed_term.astype(jnp.bfloat16), 'ch', scatter_dimensio...  37.9 us
    all_gather x1, waiting for transfers between devices, shards(): lax.all_gather(signal, 'ch', axis=0, tiled=True)  22.6 us
    unnamed x1, blocking collectives  20.2 us
  transfers between devices with their start and end apart: 10, of which 7 were waited for; matrix products, arithmetic and copies ran while one was open for 4% of the time, Pallas kernels for 0%

profile of v1, /device:TPU:1, one launch (start us, length us, event | category | flops | bytes accessed | tf_op | source)
XLA Modules:
  0.0 625.0 jit_solution(15685283141256608414)
XLA Ops:
  7.2 0.7 all-gather.8.cloned.1.call-update
  8.0 1.4 pad_maximum_fusion.4
  9.5 0.7 convert_element_type.43
  10.1 1.3 dynamic-slice.4
  12.3 20.2 %all-reduce = bf16[1536]{0:T(1024)(128)(2,1)S(1)} all-reduce(bf16[1536]{0:T(1024)(128)(2,1)S(1)} %dynamic-update-slice), channel_id=1, replica_groups=mesh['seq'=64,'ch'=8] {'ch'}, use_global_device_ids=true, to_apply=%add | all-reduce | flops 1536 | bytes 6144
  32.6 22.6 %all-gather.8.cloned.1.call-done = bf16[1536,512]{1,0:T(8,128)(2,1)} async-done(((bf16[192,512]{1,0:T(8,128)(2,1)}), bf16[1536,512]{1,0:T(8,128)(2,1)}) %all-gather.8.cloned.1.call-update) | async-done | bytes 1572880 | tf_op jit(solution)/shard_map/all_gather | solution.py:55
  55.2 1.7 copy.41
  57.2 0.5 fusion.2
  57.8 85.3 %all-gather.6.cloned.1.call-done = bf16[1536,384]{1,0:T(8,128)(2,1)} async-done(((bf16[24,384]{1,0:T(8,128)(2,1)}), bf16[1536,384]{1,0:T(8,128)(2,1)}) %all-gather.6.cloned.1.call-update) | async-done | bytes 1179664 | tf_op jit(solution)/shard_map/all_gather | solution.py:69
  143.1 2.2 fusion.6
  145.6 2.2 collective-permute-start.1
  147.7 3.4 collective-permute-start
  151.1 1.1 collective-permute-done
  152.3 0.8 fusion.33
  153.2 0.4 reshape.87
  153.6 0.4 copy.44
  154.0 2.0 convolution_select_fusion.1
  156.1 1.4 copy.58
  157.5 1.0 reshape.84
  158.5 2.0 multiply_convert_fusion.5
  160.6 1.9 collective-permute-start.3
  162.5 4.2 collective-permute-start.2
  166.8 1.1 collective-permute-done.2
  168.5 0.4 copy.50
  169.0 2.0 convolution_select_fusion
  171.0 1.4 copy.59
  172.4 1.0 reshape.85
  173.4 1.2 multiply_convert_fusion.4
  174.6 3.5 convolution_convert_fusion
  178.1 2.7 fusion.5
  181.1 0.9 copy.55
  182.0 0.4 copy.56
  182.4 2.2 fusion.49
  184.7 0.6 copy.72
  185.4 2.0 fusion
  187.4 37.9 %reduce-scatter.2.cloned.1.call-done = bf16[1536,64]{0,1:T(8,128)(2,1)} async-done(((bf16[1536,512]{0,1:T(8,128)(2,1)}), bf16[1536,64]{0,1:T(8,128)(2,1)}) %reduce-scatter.2.cloned.1.call-update) | async-done | bytes 196624 | tf_op jit(solution)/shard_map/reduce_scatter | solution.py:107
  225.3 1.3 fusion.26
  226.6 1.2 fusion.24
  228.1 0.7 copy.54
  228.8 4.7 all-to-all-start
  233.6 1.3 dynamic-slice.5
  235.5 194.4 %all-reduce.4.cloned.1.call-done = f32[1536,384]{1,0:T(8,128)} async-done(((f32[1536,384]{1,0:T(8,128)}), f32[1536,384]{1,0:T(8,128)}) %all-reduce.4.cloned.1.call-update) | async-done | bytes 2359312
  429.9 1.5 fusion.46
  431.4 86.0 %all-gather.10.cloned.1.call-done = f32[64,31,192]{2,1,0:T(8,128)} async-done(((f32[1,31,192]{2,1,0:T(8,128)}), f32[64,31,192]{2,1,0:T(8,128)}) %all-gather.10.cloned.1.call-update) | async-done | bytes 1523728 | tf_op jit(solution)/shard_map/all_gather | solution.py:89
  517.4 2.4 reduce_sum.58
  519.8 97.2 %psum.7 = f32[1536]{0:T(1024)S(1)} all-reduce(f32[1536]{0:T(1024)S(1)} %get-tuple-element.18), channel_id=1, replica_groups=mesh['seq'=64,'ch'=8] {'seq','ch'}, use_global_device_ids=true, to_apply=%region_8.0 | all-reduce | flops 1536 | bytes 12288 | tf_op jit(solution)/shard_map/psum | solution.py:118
  617.0 0.6 dynamic_slice.8
  617.7 0.8 copy.57
  (36 shorter events, 2.3 us)
Async XLA Ops:
  7.2 146.9 %copy-start = (f32[31,192]{1,0:T(8,128)S(1)}, f32[31,192]{1,0:T(8,128)}, u32[]{:S(2)}) copy-start(f32[31,192]{1,0:T(8,128)} %param.10) | copy-start | bytes 71428
  7.2 48.0 %all-gather.8.cloned.1.call-start = ((), (), s32[]{:S(2)}) async-start(), calls=%async_computation.3 | async-start | bytes 1769472 | tf_op jit(solution)/shard_map/all_gather | solution.py:55
  7.9 135.2 %all-gather.6.cloned.1.call-start = ((), (), s32[]{:S(2)}) async-start(), calls=%async_computation.2 | async-start | bytes 1198080 | tf_op jit(solution)/shard_map/all_gather | solution.py:69
  9.4 215.9 %reduce-scatter.2.cloned.1.call-start = ((), (), s32[]{:S(2)}) async-start(), calls=%async_computation.4 | async-start | bytes 1769472 | tf_op jit(solution)/shard_map/reduce_scatter | solution.py:107
  145.3 8.7 %copy-start.2 = (pred[8,68]{0,1:T(8,128)(4,1)S(1)}, pred[8,68]{0,1:T(8,128)(4,1)}, u32[]{:S(2)}) copy-start(pred[8,68]{0,1:T(8,128)(4,1)} %constant.43) | copy-start | bytes 1636
  145.6 5.6 collective-permute-start.1
  147.7 4.6 collective-permute-start
  160.6 6.2 collective-permute-start.3
  162.5 5.4 collective-permute-start.2
  178.1 3.0 copy-start.1
  178.1 251.8 %all-reduce.4.cloned.1.call-start = ((), (), s32[]{:S(2)}) async-start(), calls=%async_computation.6 | async-start | bytes 4718592
  180.8 336.6 %all-gather.10.cloned.1.call-start = ((), (), s32[]{:S(2)}) async-start(), calls=%async_computation.5 | async-start | bytes 2129920 | tf_op jit(solution)/shard_map/all_gather | solution.py:89
  228.8 388.8 %all-to-all-start = ((bf16[8,192,64]{1,2,0:T(8,128)(2,1)}), bf16[8,192,64]{1,2,0:T(8,128)(2,1)S(1)}, u32[]{:S(2)}, u32[]{:S(2)}) async-start(bf16[8,192,64]{1,2,0:T(8,128)(2,1)} %copy.54), calls=%async_computation.1 | async-start | bytes 524288 | tf_op jit(solution)/shard_map/all_to_all | solution.py:116
Sparse Core Ops, SparseCore 0:
  10.1 45.0 all-gather.7
  59.0 84.0 all-gather.5
  178.2 47.0 reduce-scatter.1
  228.6 201.2 all-reduce.3
  433.7 83.7 all-gather.9
